TPU v7x, 256 devices: a whole 4x4x8 slice. The times are simulated.
256 devices in a mesh: lon: 16 (over x, y_lo, core), lat: 16 (over y_hi, z).
Axes of the slice: x: 4, y: 4 (y_hi: 2, y_lo: 2; y = y_hi * 2 + y_lo), z: 8, core: 2. Of those that a mesh axis runs over, the one named last changes fastest.
Arguments:
- height: float32 [3072, 7200], P('lat', 'lon'), may hold values from 0.4 to 1.6
- east_wind: float32 [3072, 7200], P('lat', 'lon'), may hold values from -1.5 to 1.5
- north_wind: float32 [3072, 7200], P('lat', 'lon'), may hold values from -1.5 to 1.5
- cutoffs: int32 [512], replicated, may hold values from 1 to 64
Outputs:
- height_final: float32 [3072, 7200], P('lat', 'lon')
- east_final: float32 [3072, 7200], P('lat', 'lon')
- north_final: float32 [3072, 7200], P('lat', 'lon')
All inputs are finite; a program needn't handle non-finite values.
Results may differ from a plain program's by a relative error of at most 0.0002.
Values sent between devices are 32-bit elements; how exact they have to be, the bound alone decides.
No kernel may reach another device: no remote copies, remote signals or barrier semaphores. Data moves between devices by JAX's collectives and lax.ppermute only.
A program may use at most 128 MiB of HBM per device.

v0:
```python
import math
import jax
import jax.numpy as jnp
from jax import lax
from jax.sharding import PartitionSpec as P

NLON = 7200
LAT_ROWS = 3600
KMAX = 64
STEPS = 2
COURANT = 0.1
OMEGA_RATE = 1.5


def with_halo(value, sides, width, wrap):
    for axis, dim in sides:
        devices, length = (lax.axis_size(axis), value.shape[dim])
        up = [(i, (i + 1) % devices) for i in range(devices if wrap else devices - 1)]
        down = [(j, i) for i, j in up]
        last = lax.slice_in_dim(value, length - width, length, axis=dim)
        first = lax.slice_in_dim(value, 0, width, axis=dim)
        before = lax.ppermute(last, axis, up)
        after = lax.ppermute(first, axis, down)
        value = jnp.concatenate([before, value, after], axis=dim)
    return value


def from_behind(value, axis, by):
    devices = lax.axis_size(axis)
    return lax.ppermute(value, axis, [(i, (i + by) % devices) for i in range(devices)])


def local_table(width):
    waves = jnp.arange(KMAX + 1, dtype=jnp.int32)
    columns = lax.axis_index("lon") * width + jnp.arange(width, dtype=jnp.int32)
    phase = waves[:, None] * columns[None, :] % NLON
    angle = phase.astype(jnp.float32) * (2.0 * math.pi / NLON)
    return jnp.concatenate([jnp.cos(angle), jnp.sin(angle)], axis=0)


def spectral_weights(cut_rows):
    waves = jnp.arange(KMAX + 1, dtype=jnp.int32)
    scale = jnp.where(waves == 0, 1.0 / NLON, 2.0 / NLON).astype(jnp.float32)
    keep = (waves[None, :] <= cut_rows[:, None]).astype(jnp.float32) * scale[None, :]
    return jnp.concatenate([keep, keep], axis=1)


def project(fields, table):
    return jnp.einsum("fnw,kw->fnk", fields, table, precision=lax.Precision.HIGHEST)


def expand(coeffs, table):
    return jnp.einsum("fnk,kw->fnw", coeffs, table, precision=lax.Precision.HIGHEST)


def low_pass(fields, cut_rows, active, table):
    weights = spectral_weights(cut_rows)
    coeffs = lax.psum(project(fields, table), "lon") * weights[None]
    smooth = expand(coeffs, table)
    return jnp.where(active[None, :, None], smooth, fields)


def filter_state(state, cutoffs, table):
    rows_here = state.shape[1]
    lat_count = lax.axis_size("lat")
    lat_index = lax.axis_index("lat")
    filtered_rows = cutoffs.shape[0]
    cut_all = jnp.pad(cutoffs, (0, rows_here * lat_count - filtered_rows))
    global_rows = lat_index * rows_here + jnp.arange(rows_here, dtype=jnp.int32)
    cut_rows = lax.dynamic_slice_in_dim(cut_all, lat_index * rows_here, rows_here, 0)
    return low_pass(state, cut_rows, global_rows < filtered_rows, table)


def tendency(state, cos_all, sinlat, lon_step, lat_step):
    lat_index = lax.axis_index("lat")
    lat_count = lax.axis_size("lat")
    edge_cols = jnp.concatenate([state[:, :, :1], state[:, :, -1:]], axis=2)
    got_cols = with_halo(edge_cols, (("lon", 2),), 1, True)
    west_col = got_cols[:, :, 0:1]
    east_col = got_cols[:, :, 3:4]
    edge_rows = jnp.concatenate([state[:, :1, :], state[:, -1:, :]], axis=1)
    got_rows = with_halo(edge_rows, (("lat", 1),), 1, False)
    flips = jnp.array([1.0, -1.0, -1.0], jnp.float32)
    mirror = from_behind(state[:, 0, :], "lon", lax.axis_size("lon") // 2) * flips[:, None]
    northmost = jnp.where(lat_index == 0, mirror, got_rows[:, 0, :])
    southmost = jnp.where(lat_index == lat_count - 1, state[:, -1, :], got_rows[:, 3, :])
    corner = jnp.zeros((3, 1, 1), jnp.float32)
    top_line = jnp.concatenate([corner, northmost[:, None, :], corner], axis=2)
    bottom_line = jnp.concatenate([corner, southmost[:, None, :], corner], axis=2)
    middle_lines = jnp.concatenate([west_col, state, east_col], axis=2)
    extended = jnp.concatenate([top_line, middle_lines, bottom_line], axis=1)
    east_side = extended[:, 1:-1, 2:]
    west_side = extended[:, 1:-1, :-2]
    north_side = extended[:, :-2, 1:-1]
    south_side = extended[:, 2:, 1:-1]
    cos_north = cos_all[:-2][:, None]
    cos_south = cos_all[2:][:, None]
    coslat = cos_all[1:-1][:, None]

    def zonal_pair(east_value, west_value):
        return (east_value - west_value) * (0.5 / lon_step)

    def north_pair(north_value, south_value):
        return (north_value - south_value) * (0.5 / lat_step)

    height, east, north = (state[0], state[1], state[2])
    inv_cos = 1.0 / coslat
    turning = 2.0 * OMEGA_RATE * sinlat + east * sinlat * inv_cos
    flux_north = north_side[0] * north_side[2] * cos_north
    flux_south = south_side[0] * south_side[2] * cos_south
    rate_height = (
        -(
            zonal_pair(east_side[0] * east_side[1], west_side[0] * west_side[1])
            + north_pair(flux_north, flux_south)
        )
        * inv_cos
    )
    rate_east = (
        -east * zonal_pair(east_side[1], west_side[1]) * inv_cos
        - north * north_pair(north_side[1], south_side[1])
        + turning * north
        - zonal_pair(east_side[0], west_side[0]) * inv_cos
    )
    rate_north = (
        -east * zonal_pair(east_side[2], west_side[2]) * inv_cos
        - north * north_pair(north_side[2], south_side[2])
        - turning * east
        - north_pair(north_side[0], south_side[0])
    )
    return jnp.stack([rate_height, rate_east, rate_north], axis=0)


def shards(height, east_wind, north_wind, cutoffs):
    rows_here = height.shape[0]
    lat_index = lax.axis_index("lat")
    lat_step = math.pi / LAT_ROWS
    lon_step = 2.0 * math.pi / NLON
    time_step = COURANT * lat_step
    first_row = (lat_index * rows_here).astype(jnp.float32)
    index = first_row + jnp.arange(-1, rows_here + 1).astype(jnp.float32)
    cos_all = jnp.abs(jnp.sin((index + 0.5) * lat_step))
    sin_all = jnp.cos((index + 0.5) * lat_step)
    sinlat = sin_all[1:-1][:, None]
    table = local_table(height.shape[1])
    state = jnp.stack([height, east_wind, north_wind], axis=0)
    for step_index in range(STEPS):
        rates = tendency(state, cos_all, sinlat, lon_step, lat_step)
        middle = state + 0.5 * time_step * rates
        rates = tendency(middle, cos_all, sinlat, lon_step, lat_step)
        advanced = state + time_step * rates
        state = filter_state(advanced, cutoffs, table)
    return (state[0], state[1], state[2])


def solution(mesh):
    placed = (P("lat", "lon"), P("lat", "lon"), P("lat", "lon"), P())
    return jax.shard_map(
        shards,
        mesh=mesh,
        in_specs=placed,
        out_specs=(P("lat", "lon"), P("lat", "lon"), P("lat", "lon")),
        check_vma=False,
    )
```

profile of v0, /device:TPU:16, one launch (start us, length us, event | category | flops | bytes accessed | tf_op | source)
XLA Modules:
  0.0 351.3 jit_solution(10091914671788850582)
XLA Ops:
  9.4 2.9 collective-permute-start
  12.9 7.8 %collective-permute-start.4 = (f32[3,1,450]{2,1,0:T(1,128)}, f32[3,1,450]{2,1,0:T(1,128)}, u32[]{:S(2)}, u32[]{:S(2)}) collective-permute-start(f32[3,1,450]{2,1,0:T(1,128)} %get-tuple-element.26), channel_id=1, source_target_pairs={{1,0},{2,1},{3,2},{4,3},{5,4},{6,5},{7,6},{8,7},{9,8},{10,9},{11,1... | collective-permute-start | bytes 16208 | tf_op jit(solution)/shard_map/ppermute | solution.py:23
  23.4 1.9 collective-permute-start.3
  28.5 4.4 %collective-permute-done.3 = f32[3,1,450]{2,0,1:T(4,128)} collective-permute-done((f32[3,1,450]{2,0,1:T(4,128)}, f32[3,1,450]{2,0,1:T(4,128)}, u32[]{:S(2)}, u32[]{:S(2)}) %collective-permute-start.3) | collective-permute-done | bytes 5432 | tf_op jit(solution)/shard_map/ppermute | solution.py:22
  36.4 3.3 collective-permute-start.9
  39.6 2.8 collective-permute-start.7
  42.5 2.6 collective-permute-start.8
  45.2 2.5 collective-permute-start.5
  47.7 3.9 %collective-permute-done.8 = f32[3,1,450]{2,0,1:T(4,128)S(1)} collective-permute-done((f32[3,1,450]{2,0,1:T(4,128)S(1)}, f32[3,1,450]{2,0,1:T(4,128)S(1)}, u32[]{:S(2)}, u32[]{:S(2)}) %collective-permute-start.8) | collective-permute-done | bytes 5432 | tf_op jit(solution)/shard_map/ppermute | solution.py:22
  51.9 4.0 %collective-permute-done.6 = f32[3,192,1]{2,1,0:T(8,128)S(1)} collective-permute-done((f32[3,192,1]{2,1,0:T(8,128)S(1)}, f32[3,192,1]{2,1,0:T(8,128)S(1)}, u32[]{:S(2)}, u32[]{:S(2)}) %collective-permute-start.6) | collective-permute-done | bytes 2336 | tf_op jit(solution)/shard_map/ppermute | solution.py:22
  57.6 1.5 fusion.50
  59.0 3.2 fusion.89
  62.6 114.6 %all-reduce.4.cloned.1.call-done = f32[3,192,130]{1,2,0:T(8,128)} async-done(((f32[3,192,130]{1,2,0:T(8,128)}), f32[3,192,130]{1,2,0:T(8,128)}) %all-reduce.4.cloned.1.call-update) | async-done | bytes 299536 | tf_op jit(solution)/shard_map/psum | solution.py:58
  177.2 2.7 convolution_select_fusion.1
  180.0 5.2 %collective-permute-start.14 = (f32[3,1,450]{2,0,1:T(4,128)S(1)}, f32[3,1,450]{2,0,1:T(4,128)S(1)}, u32[]{:S(2)}, u32[]{:S(2)}) collective-permute-start(f32[3,1,450]{2,0,1:T(4,128)S(1)} %copy.96), channel_id=1, source_target_pairs={{1,0},{2,1},{3,2},{4,3},{5,4},{6,5},{7,6},{8,7},{9,8},{10,9},{11,1... | collective-permute-start | bytes 16208 | tf_op jit(solution)/shard_map/ppermute | solution.py:23
  186.5 2.5 collective-permute-start.13
  190.4 5.5 %collective-permute-done.13 = f32[3,1,450]{2,0,1:T(4,128)S(1)} collective-permute-done((f32[3,1,450]{2,0,1:T(4,128)S(1)}, f32[3,1,450]{2,0,1:T(4,128)S(1)}, u32[]{:S(2)}, u32[]{:S(2)}) %collective-permute-start.13) | collective-permute-done | bytes 5432 | tf_op jit(solution)/shard_map/ppermute | solution.py:22
  196.2 1.4 collective-permute-done.11
  200.2 7.2 %collective-permute-start.19 = (f32[3,1,450]{2,0,1:T(4,128)S(1)}, f32[3,1,450]{2,0,1:T(4,128)S(1)}, u32[]{:S(2)}, u32[]{:S(2)}) collective-permute-start(f32[3,1,450]{2,0,1:T(4,128)S(1)} %copy.95), channel_id=1, source_target_pairs={{1,0},{2,1},{3,2},{4,3},{5,4},{6,5},{7,6},{8,7},{9,8},{10,9},{11,1... | collective-permute-start | bytes 16208 | tf_op jit(solution)/shard_map/ppermute | solution.py:23
  208.8 1.9 collective-permute-start.18
  212.7 5.6 %collective-permute-done.18 = f32[3,1,450]{2,0,1:T(4,128)S(1)} collective-permute-done((f32[3,1,450]{2,0,1:T(4,128)S(1)}, f32[3,1,450]{2,0,1:T(4,128)S(1)}, u32[]{:S(2)}, u32[]{:S(2)}) %collective-permute-start.18) | collective-permute-done | bytes 5432 | tf_op jit(solution)/shard_map/ppermute | solution.py:22
  221.9 2.2 fusion.88
  224.1 116.8 %all-reduce.6.cloned.1.call-done = f32[3,192,130]{1,2,0:T(8,128)} async-done(((f32[3,192,130]{1,2,0:T(8,128)}), f32[3,192,130]{1,2,0:T(8,128)}) %all-reduce.6.cloned.1.call-update) | async-done | bytes 299536 | tf_op jit(solution)/shard_map/psum | solution.py:58
  340.9 2.5 convolution_select_fusion
  (111 shorter events, 27.8 us)
Async XLA Ops:
  7.2 170.1 %all-reduce.4.cloned.1.call-start = ((), (), s32[]{:S(2)}) async-start(), calls=%async_computation | async-start | bytes 835584 | tf_op jit(solution)/shard_map/psum | solution.py:58
  8.5 19.4 %copy-start = (f32[192,450]{1,0:T(8,128)S(1)}, f32[192,450]{1,0:T(8,128)}, u32[]{:S(2)}) copy-start(f32[192,450]{1,0:T(8,128)} %param.10) | copy-start | bytes 1036804
  8.6 19.4 %copy-start.1 = (f32[192,450]{1,0:T(8,128)S(1)}, f32[192,450]{1,0:T(8,128)}, u32[]{:S(2)}) copy-start(f32[192,450]{1,0:T(8,128)} %param.9) | copy-start | bytes 1036804
  9.4 18.6 %collective-permute-start = (f32[3,192,1]{2,1,0:T(8,128)}, f32[3,192,1]{2,1,0:T(8,128)S(1)}, u32[]{:S(2)}, u32[]{:S(2)}) collective-permute-start(f32[3,192,1]{2,1,0:T(8,128)} %get-tuple-element.29), channel_id=1, source_target_pairs={{16,0},{32,16},{48,32},{64,48},{80,64},{96,80},{112,96},{128,112},... | collective-permute-start | bytes 6920 | tf_op jit(solution)/shard_map/ppermute | solution.py:23
  12.3 15.7 %collective-permute-start.1 = (f32[3,192,1]{2,1,0:T(8,128)S(1)}, f32[3,192,1]{2,1,0:T(8,128)S(1)}, u32[]{:S(2)}, u32[]{:S(2)}) collective-permute-start(f32[3,192,1]{2,1,0:T(8,128)S(1)} %get-tuple-element.30), channel_id=1, source_target_pairs={{0,16},{16,32},{32,48},{48,64},{64,80},{80,96},{96,112},{112,128},... | collective-permute-start | bytes 6920 | tf_op jit(solution)/shard_map/ppermute | solution.py:22
  12.9 20.9 %collective-permute-start.4 = (f32[3,1,450]{2,1,0:T(1,128)}, f32[3,1,450]{2,1,0:T(1,128)}, u32[]{:S(2)}, u32[]{:S(2)}) collective-permute-start(f32[3,1,450]{2,1,0:T(1,128)} %get-tuple-element.26), channel_id=1, source_target_pairs={{1,0},{2,1},{3,2},{4,3},{5,4},{6,5},{7,6},{8,7},{9,8},{10,9},{11,1... | collective-permute-start | bytes 16208 | tf_op jit(solution)/shard_map/ppermute | solution.py:23
  22.0 6.5 %collective-permute-start.2 = (f32[3,450]{1,0:T(4,128)}, f32[3,450]{1,0:T(4,128)}, u32[]{:S(2)}, u32[]{:S(2)}) collective-permute-start(f32[3,450]{1,0:T(4,128)} %bitcast.93), channel_id=1, source_target_pairs={{0,128},{16,144},{32,160},{48,176},{64,192},{80,208},{96,224},{112... | collective-permute-start | bytes 16208 | tf_op jit(solution)/shard_map/ppermute | solution.py:30
  23.4 9.5 %collective-permute-start.3 = (f32[3,1,450]{2,0,1:T(4,128)}, f32[3,1,450]{2,0,1:T(4,128)}, u32[]{:S(2)}, u32[]{:S(2)}) collective-permute-start(f32[3,1,450]{2,0,1:T(4,128)} %copy.74), channel_id=1, source_target_pairs={{0,1},{1,2},{2,3},{3,4},{4,5},{5,6},{6,7},{7,8},{8,9},{9,10},{10,1... | collective-permute-start | bytes 16208 | tf_op jit(solution)/shard_map/ppermute | solution.py:22
  36.4 6.1 %collective-permute-start.9 = (f32[3,1,450]{2,0,1:T(4,128)S(1)}, f32[3,1,450]{2,0,1:T(4,128)S(1)}, u32[]{:S(2)}, u32[]{:S(2)}) collective-permute-start(f32[3,1,450]{2,0,1:T(4,128)S(1)} %copy.97), channel_id=1, source_target_pairs={{1,0},{2,1},{3,2},{4,3},{5,4},{6,5},{7,6},{8,7},{9,8},{10,9},{11,1... | collective-permute-start | bytes 16208 | tf_op jit(solution)/shard_map/ppermute | solution.py:23
  39.6 8.1 %collective-permute-start.7 = (f32[3,450]{1,0:T(4,128)S(1)}, f32[3,450]{1,0:T(4,128)S(1)}, u32[]{:S(2)}, u32[]{:S(2)}) collective-permute-start(f32[3,450]{1,0:T(4,128)S(1)} %bitcast.115), channel_id=1, source_target_pairs={{0,128},{16,144},{32,160},{48,176},{64,192},{80,208},{96,224},{112... | collective-permute-start | bytes 16208 | tf_op jit(solution)/shard_map/ppermute | solution.py:30
  42.5 9.2 %collective-permute-start.8 = (f32[3,1,450]{2,0,1:T(4,128)S(1)}, f32[3,1,450]{2,0,1:T(4,128)S(1)}, u32[]{:S(2)}, u32[]{:S(2)}) collective-permute-start(f32[3,1,450]{2,0,1:T(4,128)S(1)} %get-tuple-element.40), channel_id=1, source_target_pairs={{0,1},{1,2},{2,3},{3,4},{4,5},{5,6},{6,7},{7,8},{8,9},{9,10},{10,1... | collective-permute-start | bytes 16208 | tf_op jit(solution)/shard_map/ppermute | solution.py:22
  45.2 6.7 %collective-permute-start.5 = (f32[3,192,1]{2,1,0:T(8,128)S(1)}, f32[3,192,1]{2,1,0:T(8,128)S(1)}, u32[]{:S(2)}, u32[]{:S(2)}) collective-permute-start(f32[3,192,1]{2,1,0:T(8,128)S(1)} %get-tuple-element.23), channel_id=1, source_target_pairs={{16,0},{32,16},{48,32},{64,48},{80,64},{96,80},{112,96},{128,112},... | collective-permute-start | bytes 6920 | tf_op jit(solution)/shard_map/ppermute | solution.py:23
  47.7 8.3 %collective-permute-start.6 = (f32[3,192,1]{2,1,0:T(8,128)S(1)}, f32[3,192,1]{2,1,0:T(8,128)S(1)}, u32[]{:S(2)}, u32[]{:S(2)}) collective-permute-start(f32[3,192,1]{2,1,0:T(8,128)S(1)} %get-tuple-element.24), channel_id=1, source_target_pairs={{0,16},{16,32},{32,48},{48,64},{64,80},{80,96},{96,112},{112,128},... | collective-permute-start | bytes 6920 | tf_op jit(solution)/shard_map/ppermute | solution.py:22
  62.2 278.7 %all-reduce.6.cloned.1.call-start = ((), (), s32[]{:S(2)}) async-start(), calls=%async_computation.1 | async-start | bytes 835584 | tf_op jit(solution)/shard_map/psum | solution.py:58
  180.0 6.5 %collective-permute-start.14 = (f32[3,1,450]{2,0,1:T(4,128)S(1)}, f32[3,1,450]{2,0,1:T(4,128)S(1)}, u32[]{:S(2)}, u32[]{:S(2)}) collective-permute-start(f32[3,1,450]{2,0,1:T(4,128)S(1)} %copy.96), channel_id=1, source_target_pairs={{1,0},{2,1},{3,2},{4,3},{5,4},{6,5},{7,6},{8,7},{9,8},{10,9},{11,1... | collective-permute-start | bytes 16208 | tf_op jit(solution)/shard_map/ppermute | solution.py:23
  185.2 5.2 %collective-permute-start.12 = (f32[3,450]{1,0:T(4,128)S(1)}, f32[3,450]{1,0:T(4,128)S(1)}, u32[]{:S(2)}, u32[]{:S(2)}) collective-permute-start(f32[3,450]{1,0:T(4,128)S(1)} %bitcast.117), channel_id=1, source_target_pairs={{0,128},{16,144},{32,160},{48,176},{64,192},{80,208},{96,224},{112... | collective-permute-start | bytes 16208 | tf_op jit(solution)/shard_map/ppermute | solution.py:30
  186.5 9.4 %collective-permute-start.13 = (f32[3,1,450]{2,0,1:T(4,128)S(1)}, f32[3,1,450]{2,0,1:T(4,128)S(1)}, u32[]{:S(2)}, u32[]{:S(2)}) collective-permute-start(f32[3,1,450]{2,0,1:T(4,128)S(1)} %get-tuple-element.36), channel_id=1, source_target_pairs={{0,1},{1,2},{2,3},{3,4},{4,5},{5,6},{6,7},{7,8},{8,9},{9,10},{10,1... | collective-permute-start | bytes 16208 | tf_op jit(solution)/shard_map/ppermute | solution.py:22
  189.2 7.0 %collective-permute-start.10 = (f32[3,192,1]{2,1,0:T(8,128)S(1)}, f32[3,192,1]{2,1,0:T(8,128)S(1)}, u32[]{:S(2)}, u32[]{:S(2)}) collective-permute-start(f32[3,192,1]{2,1,0:T(8,128)S(1)} %get-tuple-element.19), channel_id=1, source_target_pairs={{16,0},{32,16},{48,32},{64,48},{80,64},{96,80},{112,96},{128,112},... | collective-permute-start | bytes 6920 | tf_op jit(solution)/shard_map/ppermute | solution.py:23
  189.3 8.3 %collective-permute-start.11 = (f32[3,192,1]{2,1,0:T(8,128)S(1)}, f32[3,192,1]{2,1,0:T(8,128)S(1)}, u32[]{:S(2)}, u32[]{:S(2)}) collective-permute-start(f32[3,192,1]{2,1,0:T(8,128)S(1)} %get-tuple-element.20), channel_id=1, source_target_pairs={{0,16},{16,32},{32,48},{48,64},{64,80},{80,96},{96,112},{112,128},... | collective-permute-start | bytes 6920 | tf_op jit(solution)/shard_map/ppermute | solution.py:22
  200.2 8.6 %collective-permute-start.19 = (f32[3,1,450]{2,0,1:T(4,128)S(1)}, f32[3,1,450]{2,0,1:T(4,128)S(1)}, u32[]{:S(2)}, u32[]{:S(2)}) collective-permute-start(f32[3,1,450]{2,0,1:T(4,128)S(1)} %copy.95), channel_id=1, source_target_pairs={{1,0},{2,1},{3,2},{4,3},{5,4},{6,5},{7,6},{8,7},{9,8},{10,9},{11,1... | collective-permute-start | bytes 16208 | tf_op jit(solution)/shard_map/ppermute | solution.py:23
  207.5 5.2 %collective-permute-start.17 = (f32[3,450]{1,0:T(4,128)S(1)}, f32[3,450]{1,0:T(4,128)S(1)}, u32[]{:S(2)}, u32[]{:S(2)}) collective-permute-start(f32[3,450]{1,0:T(4,128)S(1)} %bitcast.116), channel_id=1, source_target_pairs={{0,128},{16,144},{32,160},{48,176},{64,192},{80,208},{96,224},{112... | collective-permute-start | bytes 16208 | tf_op jit(solution)/shard_map/ppermute | solution.py:30
  208.8 9.5 %collective-permute-start.18 = (f32[3,1,450]{2,0,1:T(4,128)S(1)}, f32[3,1,450]{2,0,1:T(4,128)S(1)}, u32[]{:S(2)}, u32[]{:S(2)}) collective-permute-start(f32[3,1,450]{2,0,1:T(4,128)S(1)} %get-tuple-element.32), channel_id=1, source_target_pairs={{0,1},{1,2},{2,3},{3,4},{4,5},{5,6},{6,7},{7,8},{8,9},{9,10},{10,1... | collective-permute-start | bytes 16208 | tf_op jit(solution)/shard_map/ppermute | solution.py:22
  210.9 7.6 %collective-permute-start.15 = (f32[3,192,1]{2,1,0:T(8,128)S(1)}, f32[3,192,1]{2,1,0:T(8,128)S(1)}, u32[]{:S(2)}, u32[]{:S(2)}) collective-permute-start(f32[3,192,1]{2,1,0:T(8,128)S(1)} %get-tuple-element.15), channel_id=1, source_target_pairs={{16,0},{32,16},{48,32},{64,48},{80,64},{96,80},{112,96},{128,112},... | collective-permute-start | bytes 6920 | tf_op jit(solution)/shard_map/ppermute | solution.py:23
  211.2 8.4 %collective-permute-start.16 = (f32[3,192,1]{2,1,0:T(8,128)S(1)}, f32[3,192,1]{2,1,0:T(8,128)S(1)}, u32[]{:S(2)}, u32[]{:S(2)}) collective-permute-start(f32[3,192,1]{2,1,0:T(8,128)S(1)} %get-tuple-element.16), channel_id=1, source_target_pairs={{0,16},{16,32},{32,48},{48,64},{64,80},{80,96},{96,112},{112,128},... | collective-permute-start | bytes 6920 | tf_op jit(solution)/shard_map/ppermute | solution.py:22
  (10 other events, 97.2 us)
Sparse Core Ops, SparseCore 0:
  62.4 114.8 all-reduce.3
  224.2 116.6 all-reduce.5
where the time goes:
time: 352 us; the launch traced here: 351 us
  waiting for transfers between devices  261 us (74%)
  starting transfers between devices  43.8 us (12%)
  other arithmetic  15.6 us (4%)
  between operations  14.5 us (4%)
  matrix products  10.5 us (3%)
  local copies, waits for them, and re-layouts  5.62 us (2%)
    psum x2, waiting for transfers between devices, low_pass(): coeffs = lax.psum(project(fields, table), 'lon') * weights[None]  231 us
    ppermute x8, starting transfers between devices, with_halo(): after = lax.ppermute(first, axis, down)  29.4 us
    ppermute x8, waiting for transfers between devices, with_halo(): before = lax.ppermute(last, axis, up)  26 us
    ppermute x8, starting transfers between devices, with_halo(): before = lax.ppermute(last, axis, up)  9.59 us
  transfers between devices with their start and end apart: 22, of which 14 were waited for; matrix products, arithmetic and copies ran while one was open for 2% of the time, Pallas kernels for 0%

commit v1 on v0

--- a/solution.py
+++ b/solution.py
@@ -55,7 +55,7 @@
 
 def low_pass(fields, cut_rows, active, table):
     weights = spectral_weights(cut_rows)
-    coeffs = lax.psum(project(fields, table), "lon") * weights[None]
+    coeffs = jnp.sum(lax.all_gather(project(fields, table), "lon"), axis=0) * weights[None]
     smooth = expand(coeffs, table)
     return jnp.where(active[None, :, None], smooth, fields)
 

time: 352 us -> 227 us (0.64)
  waiting for transfers between devices: 261 us -> 127 us
  other arithmetic: 15.6 us -> 22.3 us
    psum x2 -> x0, waiting for transfers between devices: 231 us -> none  [low_pass(): coeffs = lax.psum(project(fields, table), 'lon') * weights[None]]
    all_gather x0 -> x2, waiting for transfers between devices: none -> 94 us  [low_pass(): lax.all_gather(project(fields, table), 'lon')]
    reduce_sum x0 -> x2, other arithmetic: none -> 7.54 us  [low_pass(): jnp.sum(lax.all_gather(project(fields, table), 'lon'), axis=0)]
  transfers between devices with their start and end apart: 22 -> 22, of which waited for: 14 -> 14; matrix products, arithmetic and copies ran while one was open for 2% -> 3% of each run, Pallas kernels for 0% -> 0%
where the time goes in v1:
time: 227 us; the launch traced here: 225 us
  waiting for transfers between devices  127 us (56%)
  starting transfers between devices  45.5 us (20%)
  other arithmetic  22.3 us (10%)
  between operations  14.7 us (6%)
  matrix products  9.67 us (4%)
  local copies, waits for them, and re-layouts  5.42 us (2%)
    all_gather x2, waiting for transfers between devices, low_pass(): lax.all_gather(project(fields, table), 'lon')  94 us
    ppermute x8, starting transfers between devices, with_halo(): after = lax.ppermute(first, axis, down)  30.7 us
    ppermute x8, waiting for transfers between devices, with_halo(): before = lax.ppermute(last, axis, up)  25.5 us
    ppermute x8, starting transfers between devices, with_halo(): before = lax.ppermute(last, axis, up)  8.29 us
    reduce_sum x2, other arithmetic, low_pass(): jnp.sum(lax.all_gather(project(fields, table), 'lon'), axis=0)  7.54 us
    ppermute x4, starting transfers between devices, from_behind(): lax.ppermute(value, axis, [(i, (i + by) % devices) for i in range(devices)])  6.2 us
    dot_general x2, matrix products, expand(): jnp.einsum('fnk,kw->fnw', coeffs, table, precision=lax.Precision.HIGHEST)  5.32 us
  transfers between devices with their start and end apart: 22, of which 14 were waited for; matrix products, arithmetic and copies ran while one was open for 3% of the time, Pallas kernels for 0%

profile of v1, /device:TPU:16, one launch (start us, length us, event | category | flops | bytes accessed | tf_op | source)
XLA Modules:
  0.0 224.8 jit_solution(17507982511708236918)
XLA Ops:
  9.2 7.5 %collective-permute-start.4 = (f32[3,1,450]{2,1,0:T(1,128)}, f32[3,1,450]{2,1,0:T(1,128)}, u32[]{:S(2)}, u32[]{:S(2)}) collective-permute-start(f32[3,1,450]{2,1,0:T(1,128)} %get-tuple-element.26), channel_id=1, source_target_pairs={{1,0},{2,1},{3,2},{4,3},{5,4},{6,5},{7,6},{8,7},{9,8},{10,9},{11,1... | collective-permute-start | bytes 16208 | tf_op jit(solution)/shard_map/ppermute | solution.py:23
  18.0 3.0 %collective-permute-start.2 = (f32[3,450]{1,0:T(4,128)}, f32[3,450]{1,0:T(4,128)}, u32[]{:S(2)}, u32[]{:S(2)}) collective-permute-start(f32[3,450]{1,0:T(4,128)} %bitcast.95), channel_id=1, source_target_pairs={{0,128},{16,144},{32,160},{48,176},{64,192},{80,208},{96,224},{112... | collective-permute-start | bytes 16208 | tf_op jit(solution)/shard_map/ppermute | solution.py:30
  21.6 1.9 collective-permute-start.3
  26.8 2.9 %collective-permute-done = f32[3,192,1]{2,1,0:T(8,128)S(1)} collective-permute-done((f32[3,192,1]{2,1,0:T(8,128)S(1)}, f32[3,192,1]{2,1,0:T(8,128)S(1)}, u32[]{:S(2)}, u32[]{:S(2)}) %collective-permute-start) | collective-permute-done | bytes 2336 | tf_op jit(solution)/shard_map/ppermute | solution.py:23
  29.7 4.1 %collective-permute-done.1 = f32[3,192,1]{2,1,0:T(8,128)S(1)} collective-permute-done((f32[3,192,1]{2,1,0:T(8,128)S(1)}, f32[3,192,1]{2,1,0:T(8,128)S(1)}, u32[]{:S(2)}, u32[]{:S(2)}) %collective-permute-start.1) | collective-permute-done | bytes 2336 | tf_op jit(solution)/shard_map/ppermute | solution.py:22
  37.8 6.7 %collective-permute-start.9 = (f32[3,1,450]{2,0,1:T(4,128)S(1)}, f32[3,1,450]{2,0,1:T(4,128)S(1)}, u32[]{:S(2)}, u32[]{:S(2)}) collective-permute-start(f32[3,1,450]{2,0,1:T(4,128)S(1)} %copy.129), channel_id=1, source_target_pairs={{1,0},{2,1},{3,2},{4,3},{5,4},{6,5},{7,6},{8,7},{9,8},{10,9},{11,1... | collective-permute-start | bytes 16208 | tf_op jit(solution)/shard_map/ppermute | solution.py:23
  45.8 1.9 collective-permute-start.8
  50.4 5.1 %collective-permute-done.8 = f32[3,1,450]{2,0,1:T(4,128)S(1)} collective-permute-done((f32[3,1,450]{2,0,1:T(4,128)S(1)}, f32[3,1,450]{2,0,1:T(4,128)S(1)}, u32[]{:S(2)}, u32[]{:S(2)}) %collective-permute-start.8) | collective-permute-done | bytes 5432 | tf_op jit(solution)/shard_map/ppermute | solution.py:22
  60.3 2.2 fusion.89
  62.9 46.6 %all-gather.5.cloned.1.call-done = f32[48,192,130]{1,2,0:T(8,128)} async-done(((f32[3,192,130]{1,2,0:T(8,128)}), f32[48,192,130]{1,2,0:T(8,128)}) %all-gather.5.cloned.1.call-update) | async-done | bytes 4792336 | tf_op jit(solution)/shard_map/all_gather | solution.py:58
  109.5 3.4 %reduce_sum.18 = f32[3,192,130]{1,2,0:T(8,128)S(1)} reduce(f32[16,3,192,130]{2,3,1,0:T(8,128)} %bitcast.117, f32[]{:T(128)} %constant.25.clone.1), dimensions={0}, to_apply=%region_0.1 | reduce | flops 1123200 | bytes 5091844 | tf_op jit(solution)/shard_map/reduce_sum | solution.py:58
  113.0 2.7 %convolution_select_fusion.1 = f32[3,192,450]{2,1,0:T(8,128)S(1)} fusion(pred[192]{0:T(512)(128)(4,1)S(1)} %add_compare_fusion, f32[3,192,130]{1,2,0:T(8,128)S(1)} %reduce_sum.18, f32[192,130]{0,1:T(8,128)S(1)} %pad_maximum_fusion.51, f32[65,450]{1,0:T(8,128)S(1)} %get-tuple-element.50, f32[65,450]{1,0:T(8,128)S(1)} %get-tuple-element.49, ...), kind=kOutput, calls=%fused_computation.13 | convolution fusion | flops 406299776 | bytes 3743952 | tf_op jit(solution)/shard_map/fnk,kw->fnw/dot_general | solution.py:53
  115.7 5.3 %collective-permute-start.14 = (f32[3,1,450]{2,0,1:T(4,128)S(1)}, f32[3,1,450]{2,0,1:T(4,128)S(1)}, u32[]{:S(2)}, u32[]{:S(2)}) collective-permute-start(f32[3,1,450]{2,0,1:T(4,128)S(1)} %copy.128), channel_id=1, source_target_pairs={{1,0},{2,1},{3,2},{4,3},{5,4},{6,5},{7,6},{8,7},{9,8},{10,9},{11,1... | collective-permute-start | bytes 16208 | tf_op jit(solution)/shard_map/ppermute | solution.py:23
  121.0 2.7 %collective-permute-start.12 = (f32[3,450]{1,0:T(4,128)S(1)}, f32[3,450]{1,0:T(4,128)S(1)}, u32[]{:S(2)}, u32[]{:S(2)}) collective-permute-start(f32[3,450]{1,0:T(4,128)S(1)} %bitcast.121), channel_id=1, source_target_pairs={{0,128},{16,144},{32,160},{48,176},{64,192},{80,208},{96,224},{112... | collective-permute-start | bytes 16208 | tf_op jit(solution)/shard_map/ppermute | solution.py:30
  123.7 1.9 collective-permute-start.13
  125.8 2.4 %collective-permute-start.10 = (f32[3,192,1]{2,1,0:T(8,128)S(1)}, f32[3,192,1]{2,1,0:T(8,128)S(1)}, u32[]{:S(2)}, u32[]{:S(2)}) collective-permute-start(f32[3,192,1]{2,1,0:T(8,128)S(1)} %get-tuple-element.19), channel_id=1, source_target_pairs={{16,0},{32,16},{48,32},{64,48},{80,64},{96,80},{112,96},{128,112},... | collective-permute-start | bytes 6920 | tf_op jit(solution)/shard_map/ppermute | solution.py:23
  128.2 4.8 %collective-permute-done.13 = f32[3,1,450]{2,0,1:T(4,128)S(1)} collective-permute-done((f32[3,1,450]{2,0,1:T(4,128)S(1)}, f32[3,1,450]{2,0,1:T(4,128)S(1)}, u32[]{:S(2)}, u32[]{:S(2)}) %collective-permute-start.13) | collective-permute-done | bytes 5432 | tf_op jit(solution)/shard_map/ppermute | solution.py:22
  133.2 3.3 %collective-permute-done.11 = f32[3,192,1]{2,1,0:T(8,128)S(1)} collective-permute-done((f32[3,192,1]{2,1,0:T(8,128)S(1)}, f32[3,192,1]{2,1,0:T(8,128)S(1)}, u32[]{:S(2)}, u32[]{:S(2)}) %collective-permute-start.11) | collective-permute-done | bytes 2336 | tf_op jit(solution)/shard_map/ppermute | solution.py:22
  139.1 6.7 %collective-permute-start.19 = (f32[3,1,450]{2,0,1:T(4,128)S(1)}, f32[3,1,450]{2,0,1:T(4,128)S(1)}, u32[]{:S(2)}, u32[]{:S(2)}) collective-permute-start(f32[3,1,450]{2,0,1:T(4,128)S(1)} %copy.127), channel_id=1, source_target_pairs={{1,0},{2,1},{3,2},{4,3},{5,4},{6,5},{7,6},{8,7},{9,8},{10,9},{11,1... | collective-permute-start | bytes 16208 | tf_op jit(solution)/shard_map/ppermute | solution.py:23
  151.0 5.5 %collective-permute-done.18 = f32[3,1,450]{2,0,1:T(4,128)S(1)} collective-permute-done((f32[3,1,450]{2,0,1:T(4,128)S(1)}, f32[3,1,450]{2,0,1:T(4,128)S(1)}, u32[]{:S(2)}, u32[]{:S(2)}) %collective-permute-start.18) | collective-permute-done | bytes 5432 | tf_op jit(solution)/shard_map/ppermute | solution.py:22
  160.5 2.2 fusion.88
  162.7 47.5 %all-gather.7.cloned.1.call-done = f32[48,192,130]{1,2,0:T(8,128)} async-done(((f32[3,192,130]{1,2,0:T(8,128)}), f32[48,192,130]{1,2,0:T(8,128)}) %all-gather.7.cloned.1.call-update) | async-done | bytes 4792336 | tf_op jit(solution)/shard_map/all_gather | solution.py:58
  210.1 4.1 %reduce_sum.19 = f32[3,192,130]{1,2,0:T(8,128)} reduce(f32[16,3,192,130]{2,3,1,0:T(8,128)} %bitcast.118, f32[]{:T(128)} %constant.25.clone.1), dimensions={0}, to_apply=%region_1.2 | reduce | flops 1123200 | bytes 5091844 | tf_op jit(solution)/shard_map/reduce_sum | solution.py:58
  214.3 2.6 %convolution_select_fusion = f32[3,192,450]{2,1,0:T(8,128)S(1)} fusion(pred[192]{0:T(512)(128)(4,1)S(1)} %copy-done.20, f32[3,192,130]{1,2,0:T(8,128)} %reduce_sum.19, f32[192,130]{0,1:T(8,128)} %copy-done.7, f32[65,450]{1,0:T(8,128)} %copy-done.5, f32[65,450]{1,0:T(8,128)} %copy-done.3, f32[3,192,450]{2,1,0:T(8,128)S(1)} %convolution_select_fusion.1, ...), kind=kOutput, calls=%fused_computation.12 | convolution fusion | flops 405781376 | bytes 3743952 | tf_op jit(solution)/shard_map/fnk,kw->fnw/dot_general | solution.py:53
  (131 shorter events, 33.1 us)
Async XLA Ops:
  7.2 102.4 %all-gather.5.cloned.1.call-start = ((), (), s32[]{:S(2)}) async-start(), calls=%async_computation | async-start | bytes 7102464 | tf_op jit(solution)/shard_map/all_gather | solution.py:58
  9.2 26.1 %collective-permute-start.4 = (f32[3,1,450]{2,1,0:T(1,128)}, f32[3,1,450]{2,1,0:T(1,128)}, u32[]{:S(2)}, u32[]{:S(2)}) collective-permute-start(f32[3,1,450]{2,1,0:T(1,128)} %get-tuple-element.26), channel_id=1, source_target_pairs={{1,0},{2,1},{3,2},{4,3},{5,4},{6,5},{7,6},{8,7},{9,8},{10,9},{11,1... | collective-permute-start | bytes 16208 | tf_op jit(solution)/shard_map/ppermute | solution.py:23
  18.0 16.3 %collective-permute-start.2 = (f32[3,450]{1,0:T(4,128)}, f32[3,450]{1,0:T(4,128)}, u32[]{:S(2)}, u32[]{:S(2)}) collective-permute-start(f32[3,450]{1,0:T(4,128)} %bitcast.95), channel_id=1, source_target_pairs={{0,128},{16,144},{32,160},{48,176},{64,192},{80,208},{96,224},{112... | collective-permute-start | bytes 16208 | tf_op jit(solution)/shard_map/ppermute | solution.py:30
  21.6 12.7 %collective-permute-start.3 = (f32[3,1,450]{2,0,1:T(4,128)}, f32[3,1,450]{2,0,1:T(4,128)}, u32[]{:S(2)}, u32[]{:S(2)}) collective-permute-start(f32[3,1,450]{2,0,1:T(4,128)} %copy.104), channel_id=1, source_target_pairs={{0,1},{1,2},{2,3},{3,4},{4,5},{5,6},{6,7},{7,8},{8,9},{9,10},{10,1... | collective-permute-start | bytes 16208 | tf_op jit(solution)/shard_map/ppermute | solution.py:22
  23.7 6.0 %collective-permute-start = (f32[3,192,1]{2,1,0:T(8,128)S(1)}, f32[3,192,1]{2,1,0:T(8,128)S(1)}, u32[]{:S(2)}, u32[]{:S(2)}) collective-permute-start(f32[3,192,1]{2,1,0:T(8,128)S(1)} %get-tuple-element.29), channel_id=1, source_target_pairs={{16,0},{32,16},{48,32},{64,48},{80,64},{96,80},{112,96},{128,112},... | collective-permute-start | bytes 6920 | tf_op jit(solution)/shard_map/ppermute | solution.py:23
  25.4 8.4 %collective-permute-start.1 = (f32[3,192,1]{2,1,0:T(8,128)S(1)}, f32[3,192,1]{2,1,0:T(8,128)S(1)}, u32[]{:S(2)}, u32[]{:S(2)}) collective-permute-start(f32[3,192,1]{2,1,0:T(8,128)S(1)} %get-tuple-element.30), channel_id=1, source_target_pairs={{0,16},{16,32},{32,48},{48,64},{64,80},{80,96},{96,112},{112,128},... | collective-permute-start | bytes 6920 | tf_op jit(solution)/shard_map/ppermute | solution.py:22
  37.8 8.0 %collective-permute-start.9 = (f32[3,1,450]{2,0,1:T(4,128)S(1)}, f32[3,1,450]{2,0,1:T(4,128)S(1)}, u32[]{:S(2)}, u32[]{:S(2)}) collective-permute-start(f32[3,1,450]{2,0,1:T(4,128)S(1)} %copy.129), channel_id=1, source_target_pairs={{1,0},{2,1},{3,2},{4,3},{5,4},{6,5},{7,6},{8,7},{9,8},{10,9},{11,1... | collective-permute-start | bytes 16208 | tf_op jit(solution)/shard_map/ppermute | solution.py:23
  45.1 67.8 %copy-start.3 = (f32[65,450]{1,0:T(8,128)}, f32[65,450]{1,0:T(8,128)S(1)}, u32[]{:S(2)}) copy-start(f32[65,450]{1,0:T(8,128)S(1)} %get-tuple-element.49) | copy-start | bytes 351004
  45.1 67.8 %copy-start.5 = (f32[65,450]{1,0:T(8,128)}, f32[65,450]{1,0:T(8,128)S(1)}, u32[]{:S(2)}) copy-start(f32[65,450]{1,0:T(8,128)S(1)} %get-tuple-element.50) | copy-start | bytes 351004
  45.1 5.2 %collective-permute-start.7 = (f32[3,450]{1,0:T(4,128)S(1)}, f32[3,450]{1,0:T(4,128)S(1)}, u32[]{:S(2)}, u32[]{:S(2)}) collective-permute-start(f32[3,450]{1,0:T(4,128)S(1)} %bitcast.119), channel_id=1, source_target_pairs={{0,128},{16,144},{32,160},{48,176},{64,192},{80,208},{96,224},{112... | collective-permute-start | bytes 16208 | tf_op jit(solution)/shard_map/ppermute | solution.py:30
  45.8 9.7 %collective-permute-start.8 = (f32[3,1,450]{2,0,1:T(4,128)S(1)}, f32[3,1,450]{2,0,1:T(4,128)S(1)}, u32[]{:S(2)}, u32[]{:S(2)}) collective-permute-start(f32[3,1,450]{2,0,1:T(4,128)S(1)} %get-tuple-element.40), channel_id=1, source_target_pairs={{0,1},{1,2},{2,3},{3,4},{4,5},{5,6},{6,7},{7,8},{8,9},{9,10},{10,1... | collective-permute-start | bytes 16208 | tf_op jit(solution)/shard_map/ppermute | solution.py:22
  47.9 7.8 %collective-permute-start.5 = (f32[3,192,1]{2,1,0:T(8,128)S(1)}, f32[3,192,1]{2,1,0:T(8,128)S(1)}, u32[]{:S(2)}, u32[]{:S(2)}) collective-permute-start(f32[3,192,1]{2,1,0:T(8,128)S(1)} %get-tuple-element.23), channel_id=1, source_target_pairs={{16,0},{32,16},{48,32},{64,48},{80,64},{96,80},{112,96},{128,112},... | collective-permute-start | bytes 6920 | tf_op jit(solution)/shard_map/ppermute | solution.py:23
  48.4 8.8 %collective-permute-start.6 = (f32[3,192,1]{2,1,0:T(8,128)S(1)}, f32[3,192,1]{2,1,0:T(8,128)S(1)}, u32[]{:S(2)}, u32[]{:S(2)}) collective-permute-start(f32[3,192,1]{2,1,0:T(8,128)S(1)} %get-tuple-element.24), channel_id=1, source_target_pairs={{0,16},{16,32},{32,48},{48,64},{64,80},{80,96},{96,112},{112,128},... | collective-permute-start | bytes 6920 | tf_op jit(solution)/shard_map/ppermute | solution.py:22
  62.5 147.7 %all-gather.7.cloned.1.call-start = ((), (), s32[]{:S(2)}) async-start(), calls=%async_computation.1 | async-start | bytes 7102464 | tf_op jit(solution)/shard_map/all_gather | solution.py:58
  115.7 8.0 %collective-permute-start.14 = (f32[3,1,450]{2,0,1:T(4,128)S(1)}, f32[3,1,450]{2,0,1:T(4,128)S(1)}, u32[]{:S(2)}, u32[]{:S(2)}) collective-permute-start(f32[3,1,450]{2,0,1:T(4,128)S(1)} %copy.128), channel_id=1, source_target_pairs={{1,0},{2,1},{3,2},{4,3},{5,4},{6,5},{7,6},{8,7},{9,8},{10,9},{11,1... | collective-permute-start | bytes 16208 | tf_op jit(solution)/shard_map/ppermute | solution.py:23
  121.0 7.2 %collective-permute-start.12 = (f32[3,450]{1,0:T(4,128)S(1)}, f32[3,450]{1,0:T(4,128)S(1)}, u32[]{:S(2)}, u32[]{:S(2)}) collective-permute-start(f32[3,450]{1,0:T(4,128)S(1)} %bitcast.121), channel_id=1, source_target_pairs={{0,128},{16,144},{32,160},{48,176},{64,192},{80,208},{96,224},{112... | collective-permute-start | bytes 16208 | tf_op jit(solution)/shard_map/ppermute | solution.py:30
  123.7 9.3 %collective-permute-start.13 = (f32[3,1,450]{2,0,1:T(4,128)S(1)}, f32[3,1,450]{2,0,1:T(4,128)S(1)}, u32[]{:S(2)}, u32[]{:S(2)}) collective-permute-start(f32[3,1,450]{2,0,1:T(4,128)S(1)} %get-tuple-element.36), channel_id=1, source_target_pairs={{0,1},{1,2},{2,3},{3,4},{4,5},{5,6},{6,7},{7,8},{8,9},{9,10},{10,1... | collective-permute-start | bytes 16208 | tf_op jit(solution)/shard_map/ppermute | solution.py:22
  125.8 7.4 %collective-permute-start.10 = (f32[3,192,1]{2,1,0:T(8,128)S(1)}, f32[3,192,1]{2,1,0:T(8,128)S(1)}, u32[]{:S(2)}, u32[]{:S(2)}) collective-permute-start(f32[3,192,1]{2,1,0:T(8,128)S(1)} %get-tuple-element.19), channel_id=1, source_target_pairs={{16,0},{32,16},{48,32},{64,48},{80,64},{96,80},{112,96},{128,112},... | collective-permute-start | bytes 6920 | tf_op jit(solution)/shard_map/ppermute | solution.py:23
  128.2 8.3 %collective-permute-start.11 = (f32[3,192,1]{2,1,0:T(8,128)S(1)}, f32[3,192,1]{2,1,0:T(8,128)S(1)}, u32[]{:S(2)}, u32[]{:S(2)}) collective-permute-start(f32[3,192,1]{2,1,0:T(8,128)S(1)} %get-tuple-element.20), channel_id=1, source_target_pairs={{0,16},{16,32},{32,48},{48,64},{64,80},{80,96},{96,112},{112,128},... | collective-permute-start | bytes 6920 | tf_op jit(solution)/shard_map/ppermute | solution.py:22
  139.1 8.0 %collective-permute-start.19 = (f32[3,1,450]{2,0,1:T(4,128)S(1)}, f32[3,1,450]{2,0,1:T(4,128)S(1)}, u32[]{:S(2)}, u32[]{:S(2)}) collective-permute-start(f32[3,1,450]{2,0,1:T(4,128)S(1)} %copy.127), channel_id=1, source_target_pairs={{1,0},{2,1},{3,2},{4,3},{5,4},{6,5},{7,6},{8,7},{9,8},{10,9},{11,1... | collective-permute-start | bytes 16208 | tf_op jit(solution)/shard_map/ppermute | solution.py:23
  145.7 5.2 %collective-permute-start.17 = (f32[3,450]{1,0:T(4,128)S(1)}, f32[3,450]{1,0:T(4,128)S(1)}, u32[]{:S(2)}, u32[]{:S(2)}) collective-permute-start(f32[3,450]{1,0:T(4,128)S(1)} %bitcast.120), channel_id=1, source_target_pairs={{0,128},{16,144},{32,160},{48,176},{64,192},{80,208},{96,224},{112... | collective-permute-start | bytes 16208 | tf_op jit(solution)/shard_map/ppermute | solution.py:30
  147.1 9.4 %collective-permute-start.18 = (f32[3,1,450]{2,0,1:T(4,128)S(1)}, f32[3,1,450]{2,0,1:T(4,128)S(1)}, u32[]{:S(2)}, u32[]{:S(2)}) collective-permute-start(f32[3,1,450]{2,0,1:T(4,128)S(1)} %get-tuple-element.32), channel_id=1, source_target_pairs={{0,1},{1,2},{2,3},{3,4},{4,5},{5,6},{6,7},{7,8},{8,9},{9,10},{10,1... | collective-permute-start | bytes 16208 | tf_op jit(solution)/shard_map/ppermute | solution.py:22
  149.1 7.5 %collective-permute-start.15 = (f32[3,192,1]{2,1,0:T(8,128)S(1)}, f32[3,192,1]{2,1,0:T(8,128)S(1)}, u32[]{:S(2)}, u32[]{:S(2)}) collective-permute-start(f32[3,192,1]{2,1,0:T(8,128)S(1)} %get-tuple-element.15), channel_id=1, source_target_pairs={{16,0},{32,16},{48,32},{64,48},{80,64},{96,80},{112,96},{128,112},... | collective-permute-start | bytes 6920 | tf_op jit(solution)/shard_map/ppermute | solution.py:23
  149.2 8.7 %collective-permute-start.16 = (f32[3,192,1]{2,1,0:T(8,128)S(1)}, f32[3,192,1]{2,1,0:T(8,128)S(1)}, u32[]{:S(2)}, u32[]{:S(2)}) collective-permute-start(f32[3,192,1]{2,1,0:T(8,128)S(1)} %get-tuple-element.16), channel_id=1, source_target_pairs={{0,16},{16,32},{32,48},{48,64},{64,80},{80,96},{96,112},{112,128},... | collective-permute-start | bytes 6920 | tf_op jit(solution)/shard_map/ppermute | solution.py:22
  (19 other events, 239.3 us)
Sparse Core Ops, SparseCore 0:
  62.6 46.9 all-gather.4
  162.8 47.2 all-gather.6
